TPU v7x, 512 devices: a whole 4x4x16 slice. The times are simulated.
512 devices in a mesh: row: 16 (over x, y), col: 32 (over z, core).
Axes of the slice: x: 4, y: 4, z: 16, core: 2. Of those that a mesh axis runs over, the one named last changes fastest.
Arguments:
- hidden: bfloat16 [2560, 7168], P('col', 'row'), may hold values from -6 to 6
- ln_gain: bfloat16 [7168], P('row'), may hold values from 0.099609375 to 1.8984375
- ln_shift: bfloat16 [7168], P('row'), may hold values from -3 to 3
- qkv_weight: bfloat16 [7168, 12288], P('row', 'col'), may hold values from -0.0625 to 0.0625
- qkv_bias: bfloat16 [12288], P('col'), may hold values from -5.351432 to 5.351432
- out_weight: bfloat16 [4096, 7168], P('row', 'col'), may hold values from -0.09375 to 0.09375
- out_bias: bfloat16 [7168], P('col'), may hold values from -3 to 3
- down_qkv: bfloat16 [64, 7168, 16], P(None, 'row'), may hold values from -0.0625 to 0.0625
- up_qkv: bfloat16 [64, 16, 12288], P(None, None, 'col'), may hold values from -1.5 to 1.5
- down_out: bfloat16 [64, 16, 4096], P(None, None, 'col'), may hold values from -0.09375 to 0.09375
- up_out: bfloat16 [64, 16, 7168], P(None, None, 'col'), may hold values from -1.5 to 1.5
- prompt_lens: int32 [16], replicated, may hold values from 1 to 80, as said below
- suffix_lens: int32 [16, 16], replicated, may hold values from 1 to 5, as said below
- group_sizes: int32 [16], replicated, may hold values from 8 to 16, as said below
- group_adapter_choice: int32 [16], replicated, may hold values from 0 to 15
- chosen: int32 [16], replicated, may hold values from 0 to 63, as said below
Outputs:
- attn_out: bfloat16 [2560, 7168], P('row', 'col')
Inputs may be any that keep to these rules, and one draw needn't show every extreme that they name: `prompt_lens`: one group, drawn from the seed, has a prompt of exactly 80 tokens, 16 requests and every suffix 5 long, so it fills all 160 slots. `suffix_lens`: entries past a group's number of requests are not used. `group_sizes`: A group's prompt and its live suffixes take at most 160 slots. `chosen`: 16 different bank indices.
All inputs are finite; a program needn't handle non-finite values.
Results may differ from a plain program's by a relative error of at most 0.012.
The roundings to bfloat16 on the way count: a program that leaves them out, or rounds other values in their place, can miss the bound.
Values may be sent and summed in bfloat16 or wider, within the bound.
No kernel may reach another device: no remote copies, remote signals or barrier semaphores. Data moves between devices by JAX's collectives and lax.ppermute only.
A program may use at most 64 MiB of HBM per device.

v0:
```python
import jax
import jax.numpy as jnp
from jax import lax
from jax.sharding import PartitionSpec as P

HEAD_SIZE = 128
GCAP = 160
WIN = 53


def group_layout(prompt, count, suffix):
    offsets = jnp.arange(GCAP, dtype=jnp.int32)
    chosen_adapter_index = jnp.arange(suffix.shape[0], dtype=jnp.int32)
    live_lens = jnp.where(chosen_adapter_index < count, suffix, 0)
    end_at = prompt + jnp.cumsum(live_lens)
    group_start_rows = end_at - live_lens
    request = jnp.sum((offsets[:, None] >= end_at[None, :]).astype(jnp.int32), axis=1)
    in_prompt = offsets < prompt
    live_rows = in_prompt | (request < count)
    group_begin_row = jnp.sum(
        jnp.where(chosen_adapter_index[None, :] == request[:, None], group_start_rows[None, :], 0),
        axis=1,
    )
    position = jnp.where(in_prompt, offsets, prompt + offsets - group_begin_row)
    request_of = jnp.where(in_prompt, -1, request)
    return (live_rows, request_of, position)


def key_mask(live_rows, request_of, position):
    shared = (request_of[None, :] == -1) | (request_of[None, :] == request_of[:, None])
    causal = position[None, :] <= position[:, None]
    within = (position[:, None] - position[None, :] < WIN) | (position[None, :] == 0)
    allowed = live_rows[:, None] & live_rows[None, :] & shared & causal & within
    first_key = jnp.arange(GCAP)[None, :] == 0
    return jnp.where(live_rows[:, None], allowed, first_key)


def attention(queries, key_rows, value_rows, allowed):
    scores = jnp.einsum("qhe,khe->hqk", queries, key_rows, preferred_element_type=jnp.float32)
    scores = jnp.where(allowed[None], scores, -1e30)
    highest = jnp.max(scores, axis=2, keepdims=True)
    weights = jnp.where(allowed[None], jnp.exp(scores - highest), 0.0)
    probs = (weights / jnp.sum(weights, axis=2, keepdims=True)).astype(jnp.bfloat16)
    mixed_rows = jnp.einsum("hqk,khe->qhe", probs, value_rows, preferred_element_type=jnp.float32)
    return mixed_rows.astype(jnp.bfloat16).reshape(queries.shape[0], -1)


def layer(
    hidden,
    ln_gain,
    ln_shift,
    qkv_weight,
    qkv_bias,
    out_weight,
    out_bias,
    down_qkv,
    up_qkv,
    down_out,
    up_out,
    prompt_lens,
    suffix_lens,
    group_sizes,
    group_adapter_choice,
    chosen,
):
    row_index = lax.axis_index("row")
    col_index = lax.axis_index("col")
    row_count = lax.axis_size("row")
    col_count = lax.axis_size("col")
    adapters = chosen[group_adapter_choice]
    own_adapter = adapters[row_index]
    tokens_here, features_here = hidden.shape
    chunk = features_here // 2
    low_rank = down_qkv.shape[2]
    head_width = qkv_weight.shape[1]
    out_rows, out_cols = out_weight.shape

    packed = jnp.concatenate(
        [qkv_weight, out_weight.reshape(features_here, -1)], axis=1
    )
    packed_full = lax.all_gather(packed, "row", axis=0, tiled=True)
    packed_full, down_rows = lax.optimization_barrier((packed_full, down_qkv[adapters]))
    down_parts = lax.all_to_all(down_rows, "row", 0, 0, tiled=True)
    down_full = down_parts.reshape(-1, low_rank)
    qkv_full = packed_full[:, :head_width]
    out_full = packed_full[:, head_width:].reshape(row_count * out_rows, out_cols)

    payload = jnp.concatenate([hidden, ln_gain[None], ln_shift[None]], axis=0)
    parity = col_index % 2
    halves = []
    for turn in range(2):
        pairs = [
            (rp * col_count + cp, (cp // 2) * col_count + 2 * rp + (turn ^ (cp % 2)))
            for rp in range(row_count)
            for cp in range(col_count)
        ]
        sent = lax.dynamic_slice_in_dim(payload, (turn ^ parity) * chunk, chunk, axis=1)
        halves.append(lax.ppermute(sent, ("row", "col"), pairs))
    first = jnp.where(parity == 0, halves[0], halves[1])
    second = jnp.where(parity == 0, halves[1], halves[0])
    mine = jnp.concatenate([first[:tokens_here], second], axis=0)
    gathered = lax.all_gather(mine, "col", axis=0, tiled=False)
    group_tokens = 2 * tokens_here
    features = gathered[:, :group_tokens, :]
    gain_full = gathered[:, group_tokens : group_tokens + 1, :]
    shift_full = gathered[:, group_tokens + 1 : group_tokens + 2, :]

    widened = features.astype(jnp.float32)
    average = jnp.mean(widened, axis=(0, 2), keepdims=True)
    centred = widened - average
    spread = jnp.mean(centred * centred, axis=(0, 2), keepdims=True)
    normed = (
        centred * lax.rsqrt(spread + 1e-05) * gain_full.astype(jnp.float32)
        + shift_full.astype(jnp.float32)
    ).astype(jnp.bfloat16)

    chunks = gathered.shape[0]
    projected = jnp.einsum(
        "ctk,ckn->tn",
        normed,
        qkv_full.reshape(chunks, chunk, head_width),
        preferred_element_type=jnp.float32,
    )
    reduced = jnp.einsum(
        "ctk,ckn->tn",
        normed,
        down_full.reshape(chunks, chunk, low_rank),
        preferred_element_type=jnp.float32,
    )
    projected = (
        projected
        + qkv_bias.astype(jnp.float32)
        + jnp.dot(
            reduced.astype(jnp.bfloat16), up_qkv[own_adapter], preferred_element_type=jnp.float32
        )
    )
    heads_here = projected.shape[1] // (3 * HEAD_SIZE)
    shaped = projected.reshape(GCAP, heads_here, 3, HEAD_SIZE)
    queries = (shaped[:, :, 0] * HEAD_SIZE ** (-0.5)).astype(jnp.bfloat16)
    key_rows = shaped[:, :, 1].astype(jnp.bfloat16)
    value_rows = shaped[:, :, 2].astype(jnp.bfloat16)
    live_rows, request_of, position = group_layout(
        prompt_lens[row_index], group_sizes[row_index], suffix_lens[row_index]
    )
    mixed_rows = attention(queries, key_rows, value_rows, key_mask(live_rows, request_of, position))
    down_here = down_out[own_adapter]
    both = lax.all_gather(
        jnp.concatenate([mixed_rows, down_here], axis=0), "col", axis=1, tiled=True
    )
    all_heads = both[:GCAP]
    down_out_full = both[GCAP:]
    reduced_out = lax.dot_general(
        all_heads, down_out_full, (((1,), (1,)), ((), ())), preferred_element_type=jnp.float32
    ).astype(jnp.bfloat16)
    combined = jnp.dot(all_heads, out_full, preferred_element_type=jnp.float32)
    result = (
        combined
        + out_bias.astype(jnp.float32)
        + jnp.dot(reduced_out, up_out[own_adapter], preferred_element_type=jnp.float32)
    )
    return (result * live_rows[:, None].astype(jnp.float32)).astype(jnp.bfloat16)


def solution(mesh):
    in_specs = (
        P("col", "row"),
        P("row"),
        P("row"),
        P("row", "col"),
        P("col"),
        P("row", "col"),
        P("col"),
        P(None, "row", None),
        P(None, None, "col"),
        P(None, None, "col"),
        P(None, None, "col"),
        P(),
        P(),
        P(),
        P(),
        P(),
    )
    out_specs = P("row", "col")
    return jax.shard_map(layer, mesh=mesh, in_specs=in_specs, out_specs=out_specs, check_vma=False)
```

profile of v0, /device:TPU:1, one launch (start us, length us, event | category | flops | bytes accessed | tf_op | source)
XLA Modules:
  0.0 300.2 jit_solution(11141923614992256735)
XLA Ops:
  6.6 0.8 broadcast_in_dim.48
  7.4 0.7 broadcast_in_dim.49
  8.1 0.9 pad_maximum_fusion.1
  9.0 0.1 constant_dynamic-slice_fusion.2
  9.1 0.7 collective-permute-start
  9.8 8.7 %collective-permute-start.1 = (bf16[82,224]{1,0:T(8,128)(2,1)S(1)}, bf16[82,224]{1,0:T(8,128)(2,1)S(1)}, u32[]{:S(2)}, u32[]{:S(2)}) collective-permute-start(bf16[82,224]{1,0:T(8,128)(2,1)S(1)} %get-tuple-element.20), channel_id=1, source_target_pairs={{0,1},{1,0},{2,33},{3,32},{4,65},{5,64},{6,97},{7,96},{8,129},{9,1... | collective-permute-start | bytes 110216 | tf_op jit(solution)/shard_map/ppermute | solution.py:98
  18.5 0.8 collective-permute-done.1
  19.4 0.7 maximum_bitcast_fusion
  20.1 1.0 copy.25
  21.1 0.3 reshape.195
  21.4 1.8 pad_maximum_fusion
  23.3 0.7 gather_fusion
  23.9 0.6 dynamic_slice.29
  25.9 0.7 dynamic_slice.32
  26.5 1.4 compare_select_fusion.3
  28.0 0.6 dynamic_slice.31
  28.6 1.3 gather_fusion.1
  30.6 0.7 dynamic-slice_bitcast_fusion
  31.3 0.7 add_reduce_fusion
  32.0 0.1 convert_reduce_fusion.1
  32.1 1.4 fusion.55
  33.5 0.1 select_reduce_fusion
  33.6 0.6 broadcast_compare_fusion
  34.2 1.3 fusion.58
  35.5 78.0 %all-gather.10.cloned.1.call-done = bf16[32,162,224]{2,1,0:T(8,128)(2,1)} async-done(((bf16[1,162,224]{2,1,0:T(8,128)(2,1)}), bf16[32,162,224]{2,1,0:T(8,128)(2,1)}) %all-gather.10.cloned.1.call-update) | async-done | bytes 2322448 | tf_op jit(solution)/shard_map/all_gather | solution.py:102
  113.6 2.4 convert_reduce_fusion
  116.0 2.7 fusion.2
  118.8 2.8 fusion.5
  121.5 72.8 %all-gather.6.cloned.1.call-done = bf16[7168,512]{1,0:T(8,128)(2,1)} async-done(((bf16[448,512]{1,0:T(8,128)(2,1)}), bf16[7168,512]{1,0:T(8,128)(2,1)}) %all-gather.6.cloned.1.call-update) | async-done | bytes 7340048 | tf_op jit(solution)/shard_map/all_gather | solution.py:81
  194.3 5.5 %slice.39 = bf16[7168,384]{1,0:T(8,128)(2,1)} slice(bf16[7168,512]{1,0:T(8,128)(2,1)} %all-gather.6.cloned.1.call-done), slice={[0:7168], [0:384]} | slice | bytes 11010048 | tf_op jit(solution)/shard_map/slice | solution.py:85
  199.8 5.0 %all-to-all-start = ((bf16[16,448,16]{1,2,0:T(8,128)(2,1)}), bf16[16,448,16]{1,2,0:T(8,128)(2,1)S(1)}, u32[]{:S(2)}, u32[]{:S(2)}) async-start(bf16[16,448,16]{1,2,0:T(8,128)(2,1)} %gather_fusion.1), calls=%async_computation | async-start | bytes 524288 | tf_op jit(solution)/shard_map/all_to_all | solution.py:83
  204.9 4.8 %fusion.10 = f32[160,384]{1,0:T(8,128)S(1)} fusion(bf16[32,160,224]{2,1,0:T(8,128)(2,1)} %fusion.5, bf16[32,224,384]{2,1,0:T(8,128)(2,1)} %bitcast.65, f32[384]{0:T(512)S(1)} %convert_element_type.72), kind=kOutput, calls=%fused_computation.16 | convolution fusion | flops 880865280 | bytes 8046080 | tf_op jit(solution)/shard_map/ctk,ckn->tn/dot_general | solution.py:118
  209.6 2.5 all-to-all-done
  212.2 0.1 copy.26
  212.3 0.2 reshape_reshape.3
  212.5 2.8 convolution_add_fusion
  215.3 0.1 reshape.197
  215.5 0.1 fusion.39
  215.6 0.2 fusion.60
  215.8 0.2 fusion.61
  216.0 0.2 fusion.38
  216.2 0.4 fusion.23
  216.6 0.6 pad_maximum_fusion.2
  217.3 0.4 slice-done
  217.7 3.2 %reshape.199 = bf16[4096,224]{1,0:T(8,128)(2,1)} reshape(bf16[7168,128]{1,0:T(8,128)(2,1)S(1)} %slice-done) | data formatting | bytes 3670016 | tf_op jit(solution)/shard_map/reshape | solution.py:86
  220.9 67.5 %all-gather.8.cloned.1.call-done = bf16[176,4096]{1,0:T(8,128)(2,1)} async-done(((bf16[176,128]{1,0:T(8,128)(2,1)}), bf16[176,4096]{1,0:T(8,128)(2,1)}) %all-gather.8.cloned.1.call-update) | async-done | bytes 1441808 | tf_op jit(solution)/shard_map/all_gather | solution.py:147
  288.4 2.1 fusion.29
  290.5 3.1 %fusion.20 = bf16[160,224]{1,0:T(8,128)(2,1)} fusion(f32[160,224]{1,0:T(8,128)S(1)} %fusion.29, bf16[4096,224]{1,0:T(8,128)(2,1)} %reshape.199, bf16[176,4096]{1,0:T(8,128)(2,1)} %all-gather.8.cloned.1.call-done, f32[160]{0:T(256)S(1)} %get-tuple-element.9, f32[224]{0:T(256)S(1)} %convert_element_type.83), kind=kOutput, calls=%fused_computation.21 | convolution fusion | flops 293744640 | bytes 3624448 | tf_op jit(solution)/shard_map/dot_general | solution.py:155
  (39 shorter events, 0.5 us)
Async XLA Ops:
  6.5 22.1 %copy-start = (bf16[64,448,16]{1,2,0:T(8,128)(2,1)S(1)}, bf16[64,448,16]{1,2,0:T(8,128)(2,1)}, u32[]{:S(2)}) copy-start(bf16[64,448,16]{1,2,0:T(8,128)(2,1)} %param.23) | copy-start | bytes 2752516
  6.5 16.7 %copy-start.3 = (bf16[384]{0:T(512)(128)(2,1)S(1)}, bf16[384]{0:T(512)(128)(2,1)}, u32[]{:S(2)}) copy-start(bf16[384]{0:T(512)(128)(2,1)} %param.20) | copy-start | bytes 2308
  6.5 16.7 %copy-start.4 = (s32[16]{0:T(128)S(1)}, s32[16]{0:T(128)}, u32[]{:S(2)}) copy-start(s32[16]{0:T(128)} %param.30) | copy-start | bytes 196
  6.5 16.7 %copy-start.1 = (s32[16]{0:T(128)S(1)}, s32[16]{0:T(128)}, u32[]{:S(2)}) copy-start(s32[16]{0:T(128)} %param.31) | copy-start | bytes 196
  6.5 19.3 %copy-start.5 = (s32[16]{0:T(128)S(1)}, s32[16]{0:T(128)}, u32[]{:S(2)}) copy-start(s32[16]{0:T(128)} %param.29) | copy-start | bytes 196
  6.5 21.5 %copy-start.6 = (s32[16]{0:T(128)S(1)}, s32[16]{0:T(128)}, u32[]{:S(2)}) copy-start(s32[16]{0:T(128)} %param.27) | copy-start | bytes 196
  6.6 107.0 %all-gather.10.cloned.1.call-start = ((), (), s32[]{:S(2)}) async-start(), calls=%async_computation.3 | async-start | bytes 2838528 | tf_op jit(solution)/shard_map/all_gather | solution.py:102
  9.1 9.4 %collective-permute-start = (bf16[82,224]{1,0:T(8,128)(2,1)S(1)}, bf16[82,224]{1,0:T(8,128)(2,1)S(1)}, u32[]{:S(2)}, u32[]{:S(2)}) collective-permute-start(bf16[82,224]{1,0:T(8,128)(2,1)S(1)} %get-tuple-element.19), channel_id=1, source_target_pairs={{0,0},{1,1},{2,32},{3,33},{4,64},{5,65},{6,96},{7,97},{8,128},{9,1... | collective-permute-start | bytes 110216 | tf_op jit(solution)/shard_map/ppermute | solution.py:98
  9.8 9.6 %collective-permute-start.1 = (bf16[82,224]{1,0:T(8,128)(2,1)S(1)}, bf16[82,224]{1,0:T(8,128)(2,1)S(1)}, u32[]{:S(2)}, u32[]{:S(2)}) collective-permute-start(bf16[82,224]{1,0:T(8,128)(2,1)S(1)} %get-tuple-element.20), channel_id=1, source_target_pairs={{0,1},{1,0},{2,33},{3,32},{4,65},{5,64},{6,97},{7,96},{8,129},{9,1... | collective-permute-start | bytes 110216 | tf_op jit(solution)/shard_map/ppermute | solution.py:98
  20.1 174.3 %all-gather.6.cloned.1.call-start = ((), (), s32[]{:S(2)}) async-start(), calls=%async_computation.1 | async-start | bytes 7798784 | tf_op jit(solution)/shard_map/all_gather | solution.py:81
  113.6 5.1 %copy-start.2 = (bf16[32,162,224]{2,1,0:T(8,128)(2,1)S(1)}, bf16[32,162,224]{2,1,0:T(8,128)(2,1)}, u32[]{:S(2)}) copy-start(bf16[32,162,224]{2,1,0:T(8,128)(2,1)} %all-gather.10.cloned.1.call-done) | copy-start | bytes 6967300
  199.8 12.3 %all-to-all-start = ((bf16[16,448,16]{1,2,0:T(8,128)(2,1)}), bf16[16,448,16]{1,2,0:T(8,128)(2,1)S(1)}, u32[]{:S(2)}, u32[]{:S(2)}) async-start(bf16[16,448,16]{1,2,0:T(8,128)(2,1)} %gather_fusion.1), calls=%async_computation | async-start | bytes 524288 | tf_op jit(solution)/shard_map/all_to_all | solution.py:83
  204.8 83.6 %all-gather.8.cloned.1.call-start = ((), (), s32[]{:S(2)}) async-start(), calls=%async_computation.2 | async-start | bytes 1486848 | tf_op jit(solution)/shard_map/all_gather | solution.py:147
  215.3 1.9 copy-start.7
  216.2 1.5 slice-start
Sparse Core Ops, SparseCore 0:
  20.2 93.3 all-gather.9
  116.6 77.6 all-gather.5
  217.4 70.9 all-gather.7
where the time goes:
time: 301 us; the launch traced here: 300 us
  waiting for transfers between devices  222 us (74%)
  other arithmetic  18 us (6%)
  local copies, waits for them, and re-layouts  17.1 us (6%)
  between operations  15.4 us (5%)
  starting transfers between devices  14.5 us (5%)
  matrix products  13.4 us (4%)
    all_gather x1, waiting for transfers between devices, layer(): gathered = lax.all_gather(mine, 'col', axis=0, tiled=False)  78 us
    all_gather x1, waiting for transfers between devices, layer(): packed_full = lax.all_gather(packed, 'row', axis=0, tiled=True)  72.8 us
    all_gather x1, waiting for transfers between devices, layer(): lax.all_gather(jnp.concatenate([mixed_rows, down_here], axis=0), 'col', a...  67.5 us
    ppermute x2, starting transfers between devices, layer(): halves.append(lax.ppermute(sent, ('row', 'col'), pairs))  9.41 us
  transfers between devices with their start and end apart: 6, of which 5 were waited for; matrix products, arithmetic and copies ran while one was open for 10% of the time, Pallas kernels for 0%

commit v1 on v0

--- a/solution.py
+++ b/solution.py
@@ -79,11 +79,10 @@
         [qkv_weight, out_weight.reshape(features_here, -1)], axis=1
     )
     packed_full = lax.all_gather(packed, "row", axis=0, tiled=True)
-    packed_full, down_rows = lax.optimization_barrier((packed_full, down_qkv[adapters]))
-    down_parts = lax.all_to_all(down_rows, "row", 0, 0, tiled=True)
-    down_full = down_parts.reshape(-1, low_rank)
     qkv_full = packed_full[:, :head_width]
     out_full = packed_full[:, head_width:].reshape(row_count * out_rows, out_cols)
+    down_parts = lax.all_to_all(down_qkv[adapters], "row", 0, 0, tiled=True)
+    down_full = down_parts.reshape(-1, low_rank)
 
     payload = jnp.concatenate([hidden, ln_gain[None], ln_shift[None]], axis=0)
     parity = col_index % 2
@@ -115,18 +114,15 @@
     ).astype(jnp.bfloat16)
 
     chunks = gathered.shape[0]
-    projected = jnp.einsum(
+    joined = jnp.concatenate([qkv_full, down_full], axis=1)
+    projected_all = jnp.einsum(
         "ctk,ckn->tn",
         normed,
-        qkv_full.reshape(chunks, chunk, head_width),
+        joined.reshape(chunks, chunk, head_width + low_rank),
         preferred_element_type=jnp.float32,
     )
-    reduced = jnp.einsum(
-        "ctk,ckn->tn",
-        normed,
-        down_full.reshape(chunks, chunk, low_rank),
-        preferred_element_type=jnp.float32,
-    )
+    projected = projected_all[:, :head_width]
+    reduced = projected_all[:, head_width:]
     projected = (
         projected
         + qkv_bias.astype(jnp.float32)

time: 301 us -> 301 us (level)
  waiting for transfers between devices: 222 us -> 190 us
  starting transfers between devices: 14.5 us -> 40.7 us
  local copies, waits for them, and re-layouts: 17.1 us -> 25.2 us
    all_gather x1, waiting for transfers between devices: 78 us -> 46.6 us  [layer(): gathered = lax.all_gather(mine, 'col', axis=0, tiled=False)]
    all_to_all x1, starting transfers between devices: 4.98 us -> 31.2 us  [layer(): down_parts = lax.all_to_all(down_qkv[adapters], 'row', 0, 0, tiled=True)]
    concatenate x0 -> x3, local copies, waits for them, and re-layouts: none -> 8.55 us  [layer(): joined = jnp.concatenate([qkv_full, down_full], axis=1)]
  transfers between devices with their start and end apart: 6 -> 6, of which waited for: 5 -> 4; matrix products, arithmetic and copies ran while one was open for 10% -> 8% of each run, Pallas kernels for 0% -> 0%
where the time goes in v1:
time: 301 us; the launch traced here: 300 us
  waiting for transfers between devices  190 us (63%)
  starting transfers between devices  40.7 us (14%)
  local copies, waits for them, and re-layouts  25.2 us (8%)
  other arithmetic  15.8 us (5%)
  between operations  15.4 us (5%)
  matrix products  12.4 us (4%)
    all_gather x1, waiting for transfers between devices, layer(): packed_full = lax.all_gather(packed, 'row', axis=0, tiled=True)  74.7 us
    all_gather x1, waiting for transfers between devices, layer(): lax.all_gather(jnp.concatenate([mixed_rows, down_here], axis=0), 'col', a...  67.9 us
    all_gather x1, waiting for transfers between devices, layer(): gathered = lax.all_gather(mine, 'col', axis=0, tiled=False)  46.6 us
    all_to_all x1, starting transfers between devices, layer(): down_parts = lax.all_to_all(down_qkv[adapters], 'row', 0, 0, tiled=True)  31.2 us
    ppermute x2, starting transfers between devices, layer(): halves.append(lax.ppermute(sent, ('row', 'col'), pairs))  9.41 us
    concatenate x3, local copies, waits for them, and re-layouts, layer(): joined = jnp.concatenate([qkv_full, down_full], axis=1)  8.55 us
  transfers between devices with their start and end apart: 6, of which 4 were waited for; matrix products, arithmetic and copies ran while one was open for 8% of the time, Pallas kernels for 0%

profile of v1, /device:TPU:1, one launch (start us, length us, event | category | flops | bytes accessed | tf_op | source)
XLA Modules:
  0.0 299.6 jit_solution(9848297046946747721)
XLA Ops:
  6.6 0.8 broadcast_in_dim.48
  7.3 0.7 broadcast_in_dim.49
  8.0 0.9 pad_maximum_fusion.1
  8.9 0.1 constant_dynamic-slice_fusion.2
  9.0 0.7 collective-permute-start
  9.7 8.7 %collective-permute-start.1 = (bf16[82,224]{1,0:T(8,128)(2,1)S(1)}, bf16[82,224]{1,0:T(8,128)(2,1)S(1)}, u32[]{:S(2)}, u32[]{:S(2)}) collective-permute-start(bf16[82,224]{1,0:T(8,128)(2,1)S(1)} %get-tuple-element.16), channel_id=1, source_target_pairs={{0,1},{1,0},{2,33},{3,32},{4,65},{5,64},{6,97},{7,96},{8,129},{9,1... | collective-permute-start | bytes 110216 | tf_op jit(solution)/shard_map/ppermute | solution.py:97
  18.5 0.8 collective-permute-done.1
  19.3 0.6 maximum_bitcast_fusion
  20.0 1.0 copy.28
  21.1 0.3 reshape.197
  21.3 1.8 pad_maximum_fusion
  23.2 0.7 gather_fusion
  23.9 1.3 gather_fusion.1
  25.1 31.2 %all-to-all-start = ((bf16[16,448,16]{1,2,0:T(8,128)(2,1)}), bf16[16,448,16]{1,2,0:T(8,128)(2,1)S(1)}, u32[]{:S(2)}, u32[]{:S(2)}) async-start(bf16[16,448,16]{1,2,0:T(8,128)(2,1)} %gather_fusion.1), calls=%async_computation | async-start | bytes 524288 | tf_op jit(solution)/shard_map/all_to_all | solution.py:84
  56.4 0.6 dynamic_slice.29
  57.0 0.6 dynamic_slice.32
  57.6 0.7 dynamic_slice.31
  59.5 1.3 compare_select_fusion.3
  61.6 0.7 dynamic-slice_bitcast_fusion
  62.2 0.8 add_reduce_fusion
  63.0 0.1 convert_reduce_fusion.1
  63.1 1.3 fusion.66
  64.4 0.1 select_reduce_fusion
  64.5 1.3 fusion.70
  65.8 0.7 broadcast_compare_fusion
  66.5 0.2 copy.29
  66.6 0.2 concatenate.24
  66.8 0.2 copy.31
  67.0 46.6 %all-gather.10.cloned.1.call-done = bf16[32,162,224]{2,1,0:T(8,128)(2,1)} async-done(((bf16[1,162,224]{2,1,0:T(8,128)(2,1)}), bf16[32,162,224]{2,1,0:T(8,128)(2,1)}) %all-gather.10.cloned.1.call-update) | async-done | bytes 2322448 | tf_op jit(solution)/shard_map/all_gather | solution.py:101
  113.6 2.3 convert_reduce_fusion
  115.9 2.7 fusion.6
  118.5 1.0 slice_convert_fusion.3
  119.6 74.7 %all-gather.6.cloned.1.call-done = bf16[7168,512]{1,0:T(8,128)(2,1)} async-done(((bf16[448,512]{1,0:T(8,128)(2,1)}), bf16[7168,512]{1,0:T(8,128)(2,1)}) %all-gather.6.cloned.1.call-update) | async-done | bytes 7340048 | tf_op jit(solution)/shard_map/all_gather | solution.py:81
  194.3 5.5 %slice.64 = bf16[7168,384]{1,0:T(8,128)(2,1)} slice(bf16[7168,512]{1,0:T(8,128)(2,1)} %all-gather.6.cloned.1.call-done), slice={[0:7168], [0:384]} | slice | bytes 11010048 | tf_op jit(solution)/shard_map/slice | solution.py:82
  199.8 8.2 %copy.30 = bf16[32,224,384]{1,2,0:T(8,128)(2,1)} copy(bf16[32,224,384]{2,1,0:T(8,128)(2,1)} %bitcast.54) | data formatting | bytes 11010048 | tf_op jit(solution)/shard_map/concatenate | solution.py:117
  208.0 5.7 %fusion.16 = f32[160,400]{1,0:T(8,128)S(1)} fusion(bf16[32,224,16]{1,2,0:T(8,128)(2,1)S(1)} %copy.31, bf16[32,224,384]{1,2,0:T(8,128)(2,1)} %copy.30, f32[32,224]{1,0:T(8,128)S(1)} %get-tuple-element.22, f32[32,224]{1,0:T(8,128)S(1)} %get-tuple-element.23, f32[160]{0:T(256)S(1)} %add_rsqrt_fusion, f32[160]{0:T(256)S(1)} %broadcast_multiply_fusion, ...), kind=kOutput, calls=%fused_computation.19 | convolution fusion | flops 935854080 | bytes 9456896 | tf_op jit(solution)/shard_map/ctk,ckn->tn/dot_general | solution.py:118
  213.7 0.9 convolution_add_fusion
  214.6 0.1 reshape.198
  214.8 0.2 fusion.72
  215.0 0.2 fusion.73
  215.2 0.2 fusion.49
  215.4 0.4 fusion.37
  215.8 0.6 pad_maximum_fusion.2
  216.5 0.2 slice-done
  216.7 3.2 %reshape.200 = bf16[4096,224]{1,0:T(8,128)(2,1)} reshape(bf16[7168,128]{1,0:T(8,128)(2,1)S(1)} %slice-done) | data formatting | bytes 3670016 | tf_op jit(solution)/shard_map/reshape | solution.py:83
  219.9 67.9 %all-gather.8.cloned.1.call-done = bf16[176,4096]{1,0:T(8,128)(2,1)} async-done(((bf16[176,128]{1,0:T(8,128)(2,1)}), bf16[176,4096]{1,0:T(8,128)(2,1)}) %all-gather.8.cloned.1.call-update) | async-done | bytes 1441808 | tf_op jit(solution)/shard_map/all_gather | solution.py:143
  287.8 2.1 fusion.42
  289.9 3.1 %fusion.34 = bf16[160,224]{1,0:T(8,128)(2,1)} fusion(f32[160,224]{1,0:T(8,128)S(1)} %fusion.42, bf16[4096,224]{1,0:T(8,128)(2,1)} %reshape.200, bf16[176,4096]{1,0:T(8,128)(2,1)} %all-gather.8.cloned.1.call-done, f32[160]{0:T(256)S(1)} %get-tuple-element.5, f32[224]{0:T(256)S(1)} %convert_element_type.80), kind=kOutput, calls=%fused_computation.29 | convolution fusion | flops 293744640 | bytes 3624448 | tf_op jit(solution)/shard_map/dot_general | solution.py:151
  (38 shorter events, 0.5 us)
Async XLA Ops:
  6.5 17.3 %copy-start = (bf16[64,448,16]{1,2,0:T(8,128)(2,1)S(1)}, bf16[64,448,16]{1,2,0:T(8,128)(2,1)}, u32[]{:S(2)}) copy-start(bf16[64,448,16]{1,2,0:T(8,128)(2,1)} %param.23) | copy-start | bytes 2752516
  6.5 16.6 %copy-start.3 = (s32[16]{0:T(128)S(1)}, s32[16]{0:T(128)}, u32[]{:S(2)}) copy-start(s32[16]{0:T(128)} %param.30) | copy-start | bytes 196
  6.5 16.6 %copy-start.1 = (s32[16]{0:T(128)S(1)}, s32[16]{0:T(128)}, u32[]{:S(2)}) copy-start(s32[16]{0:T(128)} %param.31) | copy-start | bytes 196
  6.5 107.0 %all-gather.10.cloned.1.call-start = ((), (), s32[]{:S(2)}) async-start(), calls=%async_computation.3 | async-start | bytes 2838528 | tf_op jit(solution)/shard_map/all_gather | solution.py:101
  9.0 9.4 %collective-permute-start = (bf16[82,224]{1,0:T(8,128)(2,1)S(1)}, bf16[82,224]{1,0:T(8,128)(2,1)S(1)}, u32[]{:S(2)}, u32[]{:S(2)}) collective-permute-start(bf16[82,224]{1,0:T(8,128)(2,1)S(1)} %get-tuple-element.15), channel_id=1, source_target_pairs={{0,0},{1,1},{2,32},{3,33},{4,64},{5,65},{6,96},{7,97},{8,128},{9,1... | collective-permute-start | bytes 110216 | tf_op jit(solution)/shard_map/ppermute | solution.py:97
  9.7 9.6 %collective-permute-start.1 = (bf16[82,224]{1,0:T(8,128)(2,1)S(1)}, bf16[82,224]{1,0:T(8,128)(2,1)S(1)}, u32[]{:S(2)}, u32[]{:S(2)}) collective-permute-start(bf16[82,224]{1,0:T(8,128)(2,1)S(1)} %get-tuple-element.16), channel_id=1, source_target_pairs={{0,1},{1,0},{2,33},{3,32},{4,65},{5,64},{6,97},{7,96},{8,129},{9,1... | collective-permute-start | bytes 110216 | tf_op jit(solution)/shard_map/ppermute | solution.py:97
  20.0 174.3 %all-gather.6.cloned.1.call-start = ((), (), s32[]{:S(2)}) async-start(), calls=%async_computation.1 | async-start | bytes 7798784 | tf_op jit(solution)/shard_map/all_gather | solution.py:81
  23.1 33.9 %copy-start.4 = (s32[16]{0:T(128)S(1)}, s32[16]{0:T(128)}, u32[]{:S(2)}) copy-start(s32[16]{0:T(128)} %param.29) | copy-start | bytes 196
  23.1 34.4 %copy-start.5 = (s32[16]{0:T(128)S(1)}, s32[16]{0:T(128)}, u32[]{:S(2)}) copy-start(s32[16]{0:T(128)} %param.27) | copy-start | bytes 196
  23.1 35.1 %copy-start.2 = (bf16[384]{0:T(512)(128)(2,1)S(1)}, bf16[384]{0:T(512)(128)(2,1)}, u32[]{:S(2)}) copy-start(bf16[384]{0:T(512)(128)(2,1)} %param.20) | copy-start | bytes 2308
  25.1 41.3 %all-to-all-start = ((bf16[16,448,16]{1,2,0:T(8,128)(2,1)}), bf16[16,448,16]{1,2,0:T(8,128)(2,1)S(1)}, u32[]{:S(2)}, u32[]{:S(2)}) async-start(bf16[16,448,16]{1,2,0:T(8,128)(2,1)} %gather_fusion.1), calls=%async_computation | async-start | bytes 524288 | tf_op jit(solution)/shard_map/all_to_all | solution.py:84
  56.3 231.5 %all-gather.8.cloned.1.call-start = ((), (), s32[]{:S(2)}) async-start(), calls=%async_computation.2 | async-start | bytes 1486848 | tf_op jit(solution)/shard_map/all_gather | solution.py:143
  213.7 2.8 copy-start.6
  215.2 1.5 slice-start
Sparse Core Ops, SparseCore 0:
  20.1 93.3 all-gather.9
  116.6 77.6 all-gather.5
  216.6 71.1 all-gather.7
